TPU v7x, 32 devices: a whole 2x2x4 slice. The times are simulated.
32 devices in a mesh: groups: 2 (over x), energy: 8 (over z, y), space: 2 (over core).
Axes of the slice: x: 2, y: 2, z: 4, core: 2. Of those that a mesh axis runs over, the one named last changes fastest.
Arguments:
- ham_diag: float32 [2, 2, 512, 256], P('space', None, 'groups'), parts along dimension 2, as said below
- ham_coupling: float32 [2, 2, 256, 256], P('groups'), parts along dimension 0, may hold values from -0.25 to 0.25
- sigma_shift: float32 [8, 2, 512], P('energy', 'space', 'groups'), parts along dimension 2, may hold values from -3 to 3
- sigma_width: float32 [8, 2, 512], P('energy', 'space', 'groups'), parts along dimension 2, may hold values from 0.5 to 2
- occupation: float32 [8, 2, 512], P('energy', 'space', 'groups'), parts along dimension 2, may hold values from 0 to 1
Outputs:
- polarization: float32 [16, 2, 2, 256, 256], P('groups', None, None, ('energy', 'space')), parts along dimension 0
There are 2 independent parts, one for each index of `groups`. A program takes and returns all parts, laid end to end along the dimension named above; each array names one. Nothing has to cross between parts.
Inputs may be any that keep to these rules, and one draw needn't show every extreme that they name: Each ham_diag[b, 0] is symmetric and each ham_diag[b, 1] antisymmetric.
All inputs are finite; a program needn't handle non-finite values.
Results may differ from a plain program's by a relative error of at most 0.0001.
Values sent between devices are 32-bit elements; how exact they have to be, the bound alone decides.
No kernel may reach another device: no remote copies, remote signals or barrier semaphores. Data moves between devices by JAX's collectives and lax.ppermute only.
A program may use at most 64 MiB of HBM per device.

v0:
```python
import jax
import jax.numpy as jnp
from jax import lax
from jax.sharding import PartitionSpec as P


def from_partner(shard, axis, distance):
    return lax.ppermute(shard, axis, [(i, i ^ 1 << distance) for i in range(lax.axis_size(axis))])


def dot(left, right, precision=lax.Precision.HIGHEST):
    return jnp.einsum("...ij,...jk->...ik", left, right, precision=precision)


def swap(value):
    return jnp.swapaxes(value, -1, -2)


def embed(real, imag):
    top = jnp.concatenate([real, -imag], axis=-1)
    bottom = jnp.concatenate([imag, real], axis=-1)
    return jnp.concatenate([top, bottom], axis=-2)


def stack(real, imag):
    return jnp.concatenate([real, imag], axis=-2)


def split(stacked):
    order = stacked.shape[-2] // 2
    return stacked[..., :order, :], stacked[..., order:, :]


def stacked_adjoint(real, imag):
    return stack(swap(real), -swap(imag))


def invert(matrix):
    order = matrix.shape[-1] // 2
    eye = stack(jnp.eye(order, dtype=jnp.float32), jnp.zeros((order, order), jnp.float32))
    high = lax.Precision.HIGH
    gram = jnp.einsum("...ij,...kj->...ik", matrix, matrix[..., :order, :], precision=high)
    square = dot(embed(*split(gram)), gram, high)
    square_re, square_im = split(square)
    rows = jnp.sum(jnp.abs(square_re) + jnp.abs(square_im), axis=-1)
    beta = jnp.sqrt(jnp.max(rows, axis=-1)) * 1.01 + 1e-30
    beta = beta[..., None, None]
    lower = 0.25 / beta
    alpha = 2.0 / (lower + 1.0)
    first_step = 2.0 * eye - (alpha / beta) * gram
    approx = jnp.einsum("...ji,...jk->...ik", matrix, first_step, precision=high) * (alpha / beta)
    ratio = (1.0 - lower) / (1.0 + lower)
    lower = 1.0 - ratio * ratio
    for _ in range(6):
        alpha = 2.0 / (lower + 1.0)
        product = dot(matrix, approx, high)
        approx = dot(alpha * embed(*split(approx)), 2.0 * eye - alpha * product, high)
        ratio = (1.0 - lower) / (1.0 + lower)
        lower = 1.0 - ratio * ratio

    def keep_going(state):
        _, residual, count = state
        return (residual > 7e-4) & (count < 40)

    def newton(state):
        approx, _, count = state
        rest = eye - dot(matrix, approx)
        residual = jnp.sqrt(jnp.max(jnp.sum(rest * rest, axis=(-1, -2))))
        return approx + dot(embed(*split(approx)), rest, high), residual, count + 1

    approx, _, _ = lax.while_loop(
        keep_going, newton, (approx, jnp.float32(jnp.inf), jnp.int32(0))
    )
    return approx


def body(ham_diag, ham_coupling, sigma_shift, sigma_width, occupation):
    blocks = ham_diag.shape[0]
    assert blocks == 1
    energies_here = sigma_shift.shape[0]
    order = ham_diag.shape[-1]
    side = lax.axis_index("space")
    first = side == 0
    total = energies_here * lax.axis_size("energy")
    offset = lax.axis_index("energy") * energies_here
    energy = -2.0 + 4.0 * ((offset + jnp.arange(energies_here)).astype(jnp.float32) + 0.5) / total
    identity = jnp.eye(order, dtype=jnp.float32)
    shift = sigma_shift[:, 0]
    width = sigma_width[:, 0]
    source = 2.0 * occupation[:, 0] * width
    real_part = (
        energy[:, None, None] * identity
        - ham_diag[None, 0, 0]
        - shift[:, :, None] * identity
    )
    imag_part = width[:, :, None] * identity - ham_diag[None, 0, 1]
    system = embed(real_part, imag_part)

    green_col = invert(system)
    g_re, g_im = split(green_col)
    scaled = embed(-g_im * source[:, None, :], g_re * source[:, None, :])
    far_green = from_partner(green_col, "space", 0)
    green_less = dot(scaled, stacked_adjoint(g_re, g_im))
    far_less = from_partner(green_less, "space", 0)

    link = ham_coupling[0]
    link_re = jnp.where(first, link[0], swap(link[0]))
    link_im = jnp.where(first, link[1], -swap(link[1]))
    link_embed = embed(link_re, link_im)
    link_adj = stacked_adjoint(link_re, link_im)
    high = lax.Precision.HIGH
    left_green = dot(link_embed, far_green, high)
    coupled_green = dot(embed(*split(left_green)), link_adj, high)
    left_less = dot(link_embed, far_less, high)
    coupled_less = dot(embed(*split(left_less)), link_adj, high)

    full_re, full_im = split(invert(system - embed(*split(coupled_green))))
    less_re, less_im = split(coupled_less)
    less_im = less_im + source[:, :, None] * identity
    inner = dot(embed(full_re, full_im), stack(less_re, less_im))
    lesser = dot(embed(*split(inner)), stacked_adjoint(full_re, full_im))
    lesser_re, lesser_im = split(lesser)
    greater_re = lesser_re + full_re - swap(full_re)
    greater_im = lesser_im + full_im + swap(full_im)

    chunks = lax.axis_size("energy") * lax.axis_size("space")
    row_count = order // chunks
    parts = [lesser_re, lesser_im, greater_re, greater_im]
    parts = [part.reshape((energies_here, chunks, row_count, order)) for part in parts]
    paired = jnp.moveaxis(jnp.stack(parts, axis=2), 1, 0)
    arrived = lax.all_to_all(paired, ("energy", "space"), split_axis=0, concat_axis=0, tiled=True)
    arrived = arrived.reshape(
        (lax.axis_size("energy"), lax.axis_size("space"), energies_here, 4, row_count, order)
    )
    arrived = jnp.transpose(arrived, (0, 2, 1, 3, 4, 5))
    regrouped = arrived.reshape((total, lax.axis_size("space"), 2, 2, row_count, order))
    a_re, a_im = regrouped[:, :, 0, 0], regrouped[:, :, 0, 1]
    b_re, b_im = regrouped[:, :, 1, 0], regrouped[:, :, 1, 1]
    corr_re = []
    corr_im = []
    for shift_index in range(total):
        upper_re, upper_im = a_re[shift_index:], a_im[shift_index:]
        lower_re, lower_im = b_re[: total - shift_index], b_im[: total - shift_index]
        corr_re.append(jnp.sum(upper_re * lower_re + upper_im * lower_im, axis=0))
        corr_im.append(jnp.sum(upper_im * lower_re - upper_re * lower_im, axis=0))
    corr_re = jnp.stack(corr_re, axis=0)
    corr_im = jnp.stack(corr_im, axis=0)
    return jnp.stack([-order * corr_im, order * corr_re], axis=2)


def solution(mesh):
    return jax.shard_map(
        body,
        mesh=mesh,
        in_specs=(
            P("space", None, "groups", None),
            P("groups", None, None, None),
            P("energy", "space", "groups"),
            P("energy", "space", "groups"),
            P("energy", "space", "groups"),
        ),
        out_specs=P("groups", None, None, ("energy", "space"), None),
        check_vma=False,
    )
```

profile of v0, /device:TPU:1, one launch (start us, length us, event | category | flops | bytes accessed | tf_op | source)
XLA Modules:
  0.0 90.4 jit_solution(13179423177320904063)
XLA Ops:
  0.0 1.1 %fusion.174 = (f32[1,1,256,256]{3,2,1,0:T(8,128)S(1)}, f32[1,1,256,256]{3,2,1,0:T(8,128)S(1)}) fusion(f32[1,2,256,256]{3,2,1,0:T(8,128)} %param.9), kind=kLoop, calls=%fused_computation.358 | loop fusion | bytes 1048576 | tf_op jit(solution)/shard_map/slice | solution.py:96
  13.2 0.9 %slice_negate_fusion.14 = (f32[1,256,256]{1,2,0:T(8,128)}, f32[1,256,256]{1,2,0:T(8,128)}, f32[1,256,256]{1,2,0:T(8,128)}) fusion(f32[1,512,256]{1,2,0:T(8,128)S(1)} %bitcast.390), kind=kLoop, calls=%fused_computation.346 | loop fusion | flops 65536 | bytes 1310720 | tf_op jit(solution)/shard_map/neg | solution.py:20
  14.2 1.4 %select_subtract_fusion.7 = f32[512,256]{0,1:T(8,128)} fusion(f32[512,256]{0,1:T(8,128)S(1)} %fusion.38, pred[256,256]{0,1:T(32,128)(4,1)S(1)} %iota_compare_fusion, f32[]{:T(128)} %bitcast.19, f32[1,256,256]{1,2,0:T(8,128)S(1)} %get-tuple-element.247, f32[1,256,256]{1,2,0:T(8,128)S(1)} %get-tuple-element.130, f32[1,256,256]{1,2,0:T(8,128)S(1)} %get-tuple-element.129), kind=kOutput, calls=%fused_computation.37 | convolution fusion | flops 403832832 | bytes 1900548 | tf_op jit(solution)/shard_map/...ij,...jk->...ik/dot_general | solution.py:12
  16.2 0.7 copy-done.2
  17.0 1.2 %maximum_bitcast_fusion.31 = (f32[256,512]{0,1:T(8,128)S(1)}, f32[256,512]{0,1:T(8,128)S(1)}) fusion(f32[1,256,256]{1,2,0:T(8,128)S(1)} %copy-done.2, f32[1,256,256]{1,2,0:T(8,128)} %get-tuple-element.193, f32[1,256,256]{1,2,0:T(8,128)S(1)} %copy-done.3), kind=kLoop, calls=%fused_computation.193 | loop fusion | flops 262144 | bytes 1835008 | tf_op jit(solution)/shard_map/concatenate | solution.py:22
  18.2 1.0 %convolution_bitcast_fusion.11 = f32[1,512,256]{2,1,0:T(8,128)S(1)} fusion(f32[512,256]{0,1:T(8,128)S(1)} %copy-done.4, f32[256,512]{0,1:T(8,128)S(1)} %get-tuple-element.232, f32[256,512]{0,1:T(8,128)S(1)} %get-tuple-element.231, f32[]{:T(128)} %bitcast.19), kind=kOutput, calls=%fused_computation.67 | convolution fusion | flops 403177472 | bytes 2097156 | tf_op jit(solution)/shard_map/...ij,...jk->...ik/dot_general | solution.py:12
  19.2 3.3 %while.24 = (f32[1,512,256]{2,1,0:T(8,128)S(1)}, f32[]{:T(128)}, s32[]{:T(128)}, f32[1,512,512]{2,1,0:T(8,128)S(1)}, f32[512,256]{1,0:T(8,128)S(1)}, /*index=5*/s32[]{:T(128)}) while((f32[1,512,256]{2,1,0:T(8,128)S(1)}, f32[]{:T(128)}, s32[]{:T(128)}, f32[1,512,512]{2,1,0:T(8,128)S(1)}, f32[512,256]{1,0:T(8,128)S(1)}, ...), condition=%wide.region_4.5_spmd, body=%wide.region_2.4_spmd.sunk | while | flops 1209335808 | bytes 6291549 | solution.py:71
  19.2 1.6 %multiply_reduce_fusion.4 = (f32[]{:T(128)}, f32[512,256]{1,0:T(8,128)S(1)}) fusion(f32[512,256]{1,0:T(8,128)S(1)} %get-tuple-element.344, f32[1,512,256]{2,1,0:T(8,128)S(1)} %get-tuple-element.334, f32[1,512,512]{2,1,0:T(8,128)S(1)} %get-tuple-element.343), kind=kOutput, calls=%fused_computation.12.clone.1 | convolution fusion | flops 805699584 | bytes 2621444 | tf_op jit(solution)/shard_map/while/body/...ij,...jk->...ik/dot_general | solution.py:12
  20.8 0.7 fusion.216
  23.3 1.8 %convolution_bitcast_fusion.6 = f32[1,512,256]{2,1,0:T(8,128)} fusion(f32[1,256,256]{2,1,0:T(8,128)S(1)} %get-tuple-element.158, f32[1,256,256]{2,1,0:T(8,128)S(1)} %get-tuple-element.160, f32[1,256,256]{2,1,0:T(8,128)S(1)} %get-tuple-element.159, f32[1,256,256]{1,2,0:T(8,128)S(1)} %get-tuple-element.157, f32[1,256,256]{1,2,0:T(8,128)S(1)} %get-tuple-element.156), kind=kOutput, calls=%fused_computation.62 | convolution fusion | flops 806223872 | bytes 1835008 | tf_op jit(solution)/shard_map/...ij,...jk->...ik/dot_general | solution.py:12
  26.3 2.1 %convolution_bitcast_fusion.10 = f32[1,512,256]{1,2,0:T(8,128)S(1)} fusion(f32[256,256]{1,0:T(8,128)S(1)} %get-tuple-element.212, f32[256,256]{1,0:T(8,128)S(1)} %get-tuple-element.128, f32[256,256]{1,0:T(8,128)S(1)} %neg.110, f32[1,512,256]{2,1,0:T(8,128)} %collective-permute-done), kind=kOutput, calls=%fused_computation.66 | convolution fusion | flops 403439616 | bytes 1835008 | tf_op jit(solution)/shard_map/...ij,...jk->...ik/dot_general | solution.py:12
  29.6 0.7 copy-done
  33.6 1.6 %copy.61 = f32[1,512,512]{2,1,0:T(8,128)S(1)} copy(f32[1,512,512]{1,2,0:T(8,128)} %copy-done) | data formatting | bytes 2097152 | tf_op jit(solution)/shard_map/while | solution.py:71
  35.1 2.3 %convolution_bitcast_fusion.5 = f32[1,512,256]{1,2,0:T(8,128)S(1)} fusion(f32[256,256]{1,0:T(8,128)} %copy-done.10, f32[256,256]{1,0:T(8,128)S(1)} %get-tuple-element.128, f32[256,256]{1,0:T(8,128)} %copy-done.7, f32[1,512,256]{2,1,0:T(8,128)} %collective-permute-done.1), kind=kOutput, calls=%fused_computation.61 | convolution fusion | flops 403439616 | bytes 1835008 | tf_op jit(solution)/shard_map/...ij,...jk->...ik/dot_general | solution.py:12
  37.5 0.9 slice_negate_fusion.4
  44.0 0.8 fusion.64
  47.1 1.0 %convolution_bitcast_fusion.7 = f32[1,512,256]{2,1,0:T(8,128)S(1)} fusion(f32[512,256]{0,1:T(8,128)S(1)} %select_subtract_fusion, f32[256,512]{0,1:T(8,128)S(1)} %get-tuple-element.218, f32[256,512]{0,1:T(8,128)S(1)} %get-tuple-element.217, f32[]{:T(128)} %bitcast.64), kind=kOutput, calls=%fused_computation.63 | convolution fusion | flops 403177472 | bytes 2097156 | tf_op jit(solution)/shard_map/...ij,...jk->...ik/dot_general | solution.py:12
  48.2 3.0 %while.25 = (f32[1,512,256]{2,1,0:T(8,128)S(1)}, f32[]{:T(128)}, s32[]{:T(128)}, f32[1,512,512]{2,1,0:T(8,128)S(1)}, f32[512,256]{1,0:T(8,128)S(1)}, /*index=5*/s32[]{:T(128)}) while((f32[1,512,256]{2,1,0:T(8,128)S(1)}, f32[]{:T(128)}, s32[]{:T(128)}, f32[1,512,512]{2,1,0:T(8,128)S(1)}, f32[512,256]{1,0:T(8,128)S(1)}, ...), condition=%wide.region_9.0_spmd, body=%wide.region_7.0_spmd.sunk | while | flops 1209335808 | bytes 6291549 | solution.py:71
  48.2 1.6 %multiply_reduce_fusion.5 = (f32[]{:T(128)}, f32[512,256]{1,0:T(8,128)S(1)}) fusion(f32[512,256]{1,0:T(8,128)S(1)} %get-tuple-element.362, f32[1,512,256]{2,1,0:T(8,128)S(1)} %get-tuple-element.352, f32[1,512,512]{2,1,0:T(8,128)S(1)} %get-tuple-element.361), kind=kOutput, calls=%fused_computation.27.clone.1 | convolution fusion | flops 805699584 | bytes 2621444 | tf_op jit(solution)/shard_map/while/body/...ij,...jk->...ik/dot_general | solution.py:12
  49.8 0.7 fusion.218
  53.1 1.1 %convolution_bitcast_fusion.3 = f32[1,512,256]{1,2,0:T(8,128)S(1)} fusion(f32[1,256,256]{2,1,0:T(8,128)S(1)} %get-tuple-element.163, f32[1,256,256]{2,1,0:T(8,128)S(1)} %get-tuple-element.162, f32[1,256,256]{2,1,0:T(8,128)S(1)} %get-tuple-element.161, f32[1,256,256]{1,2,0:T(8,128)S(1)} %get-tuple-element.152, f32[1,256,256]{1,2,0:T(8,128)S(1)} %get-tuple-element.151), kind=kOutput, calls=%fused_computation.59 | convolution fusion | flops 806223872 | bytes 1835008 | tf_op jit(solution)/shard_map/...ij,...jk->...ik/dot_general | solution.py:12
  54.3 1.8 %convolution_bitcast_fusion.2 = f32[1,512,256]{2,1,0:T(8,128)S(1)} fusion(f32[1,256,256]{1,2,0:T(8,128)S(1)} %get-tuple-element.150, f32[1,256,256]{1,2,0:T(8,128)S(1)} %get-tuple-element.149, f32[1,256,256]{1,2,0:T(8,128)S(1)} %get-tuple-element.148, f32[1,256,256]{2,1,0:T(8,128)S(1)} %bitcast_negate_fusion, f32[1,256,256]{2,1,0:T(8,128)S(1)} %bitcast.395), kind=kOutput, calls=%fused_computation.58 | convolution fusion | flops 806223872 | bytes 1835008 | tf_op jit(solution)/shard_map/...ij,...jk->...ik/dot_general | solution.py:12
  56.3 32.5 %all_to_all.5 = f32[16,1,4,16,256]{4,3,2,1,0:T(8,128)S(1)} all-to-all(f32[16,1,4,16,256]{4,3,2,1,0:T(8,128)S(1)} %maximum_bitcast_fusion.18), channel_id=1, replica_groups=mesh['groups'=2,'energy'=8,'space'=2] {'energy','space'}, dimensions={0} | all-to-all | bytes 2097152 | tf_op jit(solution)/shard_map/all_to_all | solution.py:131
  89.6 0.8 copy.76
  (145 shorter events, 26.9 us)
Async XLA Ops:
  1.2 0.7 copy-start.13
  1.4 0.7 copy-start.12
  15.9 1.0 %copy-start.2 = (f32[1,256,256]{1,2,0:T(8,128)S(1)}, f32[1,256,256]{1,2,0:T(8,128)}, u32[]{:S(2)}) copy-start(f32[1,256,256]{1,2,0:T(8,128)} %get-tuple-element.191) | copy-start | bytes 786436
  15.9 1.0 %copy-start.3 = (f32[1,256,256]{1,2,0:T(8,128)S(1)}, f32[1,256,256]{1,2,0:T(8,128)}, u32[]{:S(2)}) copy-start(f32[1,256,256]{1,2,0:T(8,128)} %get-tuple-element.192) | copy-start | bytes 786436
  17.0 1.2 %copy-start.4 = (f32[512,256]{0,1:T(8,128)S(1)}, f32[512,256]{0,1:T(8,128)}, u32[]{:S(2)}) copy-start(f32[512,256]{0,1:T(8,128)} %select_subtract_fusion.7) | copy-start | bytes 1572868
  22.5 0.7 copy-start.14
  22.5 3.2 %collective-permute-start = (f32[1,512,256]{2,1,0:T(8,128)S(1)}, f32[1,512,256]{2,1,0:T(8,128)}, u32[]{:S(2)}, u32[]{:S(2)}) collective-permute-start(f32[1,512,256]{2,1,0:T(8,128)S(1)} %get-tuple-element.59), channel_id=1, source_target_pairs={{0,1},{1,0},{2,3},{3,2},{4,5},{5,4},{6,7},{7,6},{8,9},{9,8},{10,11... | collective-permute-start | bytes 1572872 | tf_op jit(solution)/shard_map/ppermute | solution.py:8
  23.3 1.9 %copy-start.1 = (f32[1,2,256,256]{3,2,1,0:T(8,128)S(1)}, f32[1,2,256,256]{3,2,1,0:T(8,128)}, u32[]{:S(2)}) copy-start(f32[1,2,256,256]{3,2,1,0:T(8,128)} %param.10) | copy-start | bytes 1572868
  25.1 10.0 %collective-permute-start.1 = (f32[1,512,256]{2,1,0:T(8,128)}, f32[1,512,256]{2,1,0:T(8,128)}, u32[]{:S(2)}, u32[]{:S(2)}) collective-permute-start(f32[1,512,256]{2,1,0:T(8,128)} %convolution_bitcast_fusion.6), channel_id=1, source_target_pairs={{0,1},{1,0},{2,3},{3,2},{4,5},{5,4},{6,7},{7,6},{8,9},{9,8},{10,11... | collective-permute-start | bytes 1572872 | tf_op jit(solution)/shard_map/ppermute | solution.py:8
  25.5 3.0 %copy-start.8 = (f32[256,256]{0,1:T(8,128)}, f32[256,256]{0,1:T(8,128)S(1)}, u32[]{:S(2)}) copy-start(f32[256,256]{0,1:T(8,128)S(1)} %get-tuple-element.127) | copy-start | bytes 786436
  25.5 3.0 %copy-start.10 = (f32[256,256]{1,0:T(8,128)}, f32[256,256]{1,0:T(8,128)S(1)}, u32[]{:S(2)}) copy-start(f32[256,256]{1,0:T(8,128)S(1)} %get-tuple-element.212) | copy-start | bytes 786436
  25.6 0.8 copy-start.7
  29.4 1.0 %copy-start = (f32[1,512,512]{1,2,0:T(8,128)}, f32[1,512,512]{1,2,0:T(8,128)S(1)}, u32[]{:S(2)}) copy-start(f32[1,512,512]{1,2,0:T(8,128)S(1)} %maximum_subtract_fusion.1) | copy-start | bytes 3145732
  51.2 1.0 %copy-start.9 = (f32[256,256]{0,1:T(8,128)S(1)}, f32[256,256]{0,1:T(8,128)}, u32[]{:S(2)}) copy-start(f32[256,256]{0,1:T(8,128)} %copy-done.8) | copy-start | bytes 786436
  51.2 1.0 %copy-start.11 = (f32[256,256]{1,0:T(8,128)S(1)}, f32[256,256]{1,0:T(8,128)}, u32[]{:S(2)}) copy-start(f32[256,256]{1,0:T(8,128)} %copy-done.10) | copy-start | bytes 786436
  51.4 1.0 %copy-start.5 = (f32[1,256,256]{1,2,0:T(8,128)S(1)}, f32[1,256,256]{1,2,0:T(8,128)}, u32[]{:S(2)}) copy-start(f32[1,256,256]{1,2,0:T(8,128)} %get-tuple-element.154) | copy-start | bytes 786436
  51.4 1.1 %copy-start.6 = (f32[1,256,256]{1,2,0:T(8,128)S(1)}, f32[1,256,256]{1,2,0:T(8,128)}, u32[]{:S(2)}) copy-start(f32[1,256,256]{1,2,0:T(8,128)} %get-tuple-element.155) | copy-start | bytes 786436
where the time goes:
time: 90.8 us; the launch traced here: 90.4 us
  matrix products  35.2 us (39%)
  blocking collectives  32.5 us (36%)
  local copies, waits for them, and re-layouts  9.27 us (10%)
  other arithmetic  8.14 us (9%)
  between operations  3.71 us (4%)
  loops' own time  1.53 us (2%)
    dot_general x37, matrix products, dot(): return jnp.einsum('...ij,...jk->...ik', left, right, precision=precision)  32.7 us
    all_to_all x1, blocking collectives, body(): lax.all_to_all(paired, ('energy', 'space'), split_axis=0, concat_axis=0,...  32.5 us
    unnamed x47, local copies, waits for them, and re-layouts  4.87 us
    neg x23, other arithmetic, embed(): top = jnp.concatenate([real, -imag], axis=-1)  3.02 us
    concatenate x15, other arithmetic, embed(): return jnp.concatenate([top, bottom], axis=-2)  2.33 us
    while x3, local copies, waits for them, and re-layouts, invert(): lax.while_loop(keep_going, newton, (approx, jnp.float32(jnp.inf), jnp.int...  2.08 us
  transfers between devices with their start and end apart: 2, of which 0 were waited for; matrix products, arithmetic and copies ran while one was open for 10% of the time, Pallas kernels for 0%

commit v1 on v0

--- a/solution.py
+++ b/solution.py
@@ -100,13 +100,13 @@
     g_re, g_im = split(green_col)
     scaled = embed(-g_im * source[:, None, :], g_re * source[:, None, :])
     far_green = from_partner(green_col, "space", 0)
-    green_less = dot(scaled, stacked_adjoint(g_re, g_im))
+    green_less = dot(scaled, stacked_adjoint(g_re, g_im), lax.Precision.HIGH)
     far_less = from_partner(green_less, "space", 0)
 
     link = ham_coupling[0]
     link_re = jnp.where(first, link[0], swap(link[0]))
     link_im = jnp.where(first, link[1], -swap(link[1]))
-    link_embed = embed(link_re, link_im)
+    link_embed = lax.optimization_barrier(embed(link_re, link_im))
     link_adj = stacked_adjoint(link_re, link_im)
     high = lax.Precision.HIGH
     left_green = dot(link_embed, far_green, high)

time: 90.8 us -> 91.8 us (1.011)
  other arithmetic: 8.14 us -> 9.09 us
    unnamed x47 -> x45, local copies, waits for them, and re-layouts: 4.87 us -> 3.46 us
    while x3, local copies, waits for them, and re-layouts: 2.08 us -> 3.31 us  [invert(): lax.while_loop(keep_going, newton, (approx, jnp.float32(jnp.inf), jnp.int...]
    concatenate x15 -> x16, other arithmetic: 2.33 us -> 3.42 us  [embed(): return jnp.concatenate([top, bottom], axis=-2)]
where the time goes in v1:
time: 91.8 us; the launch traced here: 91.4 us
  matrix products  35.4 us (39%)
  blocking collectives  32.5 us (35%)
  local copies, waits for them, and re-layouts  9.1 us (10%)
  other arithmetic  9.09 us (10%)
  between operations  3.63 us (4%)
  loops' own time  1.61 us (2%)
    dot_general x37, matrix products, dot(): return jnp.einsum('...ij,...jk->...ik', left, right, precision=precision)  32.8 us
    all_to_all x1, blocking collectives, body(): lax.all_to_all(paired, ('energy', 'space'), split_axis=0, concat_axis=0,...  32.5 us
    unnamed x45, local copies, waits for them, and re-layouts  3.46 us
    concatenate x16, other arithmetic, embed(): return jnp.concatenate([top, bottom], axis=-2)  3.42 us
    while x3, local copies, waits for them, and re-layouts, invert(): lax.while_loop(keep_going, newton, (approx, jnp.float32(jnp.inf), jnp.int...  3.31 us
    neg x23, other arithmetic, embed(): top = jnp.concatenate([real, -imag], axis=-1)  2.92 us
  transfers between devices with their start and end apart: 2, of which 0 were waited for; matrix products, arithmetic and copies ran while one was open for 10% of the time, Pallas kernels for 0%

profile of v1, /device:TPU:1, one launch (start us, length us, event | category | flops | bytes accessed | tf_op | source)
XLA Modules:
  0.0 91.4 jit_solution(13900086460156975691)
XLA Ops:
  0.0 1.1 %fusion.172 = (f32[1,1,256,256]{3,2,1,0:T(8,128)S(1)}, f32[1,1,256,256]{3,2,1,0:T(8,128)S(1)}) fusion(f32[1,2,256,256]{3,2,1,0:T(8,128)} %param.9), kind=kLoop, calls=%fused_computation.356 | loop fusion | bytes 1048576 | tf_op jit(solution)/shard_map/slice | solution.py:96
  5.2 1.1 %maximum_maximum_fusion = f32[1,512,512]{1,2,0:T(8,128)} fusion(f32[1,256,256]{1,2,0:T(8,128)S(1)} %get-tuple-element.247, f32[1,256,256]{1,2,0:T(8,128)S(1)} %get-tuple-element.130, f32[1,256,256]{1,2,0:T(8,128)S(1)} %get-tuple-element.129), kind=kLoop, calls=%fused_computation.70 | loop fusion | flops 786432 | bytes 1835008 | tf_op jit(solution)/shard_map/concatenate | solution.py:22
  14.1 0.8 slice_negate_fusion.14
  15.0 1.4 %select_subtract_fusion.7 = f32[512,256]{0,1:T(8,128)} fusion(f32[512,256]{0,1:T(8,128)S(1)} %fusion.38, pred[256,256]{0,1:T(32,128)(4,1)S(1)} %iota_compare_fusion, f32[]{:T(128)} %bitcast.19, f32[1,256,256]{1,2,0:T(8,128)S(1)} %get-tuple-element.247, f32[1,256,256]{1,2,0:T(8,128)S(1)} %get-tuple-element.130, f32[1,256,256]{1,2,0:T(8,128)S(1)} %get-tuple-element.129), kind=kOutput, calls=%fused_computation.37 | convolution fusion | flops 403832832 | bytes 1900548 | tf_op jit(solution)/shard_map/...ij,...jk->...ik/dot_general | solution.py:12
  16.4 1.6 %copy.50 = f32[1,512,512]{2,1,0:T(8,128)S(1)} copy(f32[1,512,512]{1,2,0:T(8,128)} %maximum_maximum_fusion) | data formatting | bytes 2097152 | tf_op jit(solution)/shard_map/while | solution.py:71
  18.2 1.2 %maximum_bitcast_fusion.31 = (f32[256,512]{0,1:T(8,128)S(1)}, f32[256,512]{0,1:T(8,128)S(1)}) fusion(f32[1,256,256]{1,2,0:T(8,128)S(1)} %get-tuple-element.191, f32[1,256,256]{1,2,0:T(8,128)} %get-tuple-element.193, f32[1,256,256]{1,2,0:T(8,128)S(1)} %get-tuple-element.192), kind=kLoop, calls=%fused_computation.193 | loop fusion | flops 262144 | bytes 1835008 | tf_op jit(solution)/shard_map/concatenate | solution.py:22
  19.4 1.0 %convolution_bitcast_fusion.11 = f32[1,512,256]{2,1,0:T(8,128)S(1)} fusion(f32[512,256]{0,1:T(8,128)S(1)} %copy-done.5, f32[256,512]{0,1:T(8,128)S(1)} %get-tuple-element.232, f32[256,512]{0,1:T(8,128)S(1)} %get-tuple-element.231, f32[]{:T(128)} %bitcast.19), kind=kOutput, calls=%fused_computation.67 | convolution fusion | flops 403177472 | bytes 2097156 | tf_op jit(solution)/shard_map/...ij,...jk->...ik/dot_general | solution.py:12
  20.4 3.3 %while.24 = (f32[1,512,256]{2,1,0:T(8,128)S(1)}, f32[]{:T(128)}, s32[]{:T(128)}, f32[1,512,512]{2,1,0:T(8,128)S(1)}, f32[512,256]{1,0:T(8,128)S(1)}, /*index=5*/s32[]{:T(128)}) while((f32[1,512,256]{2,1,0:T(8,128)S(1)}, f32[]{:T(128)}, s32[]{:T(128)}, f32[1,512,512]{2,1,0:T(8,128)S(1)}, f32[512,256]{1,0:T(8,128)S(1)}, ...), condition=%wide.region_4.5_spmd, body=%wide.region_2.4_spmd.sunk | while | flops 1209335808 | bytes 6291549 | solution.py:71
  20.4 1.6 %multiply_reduce_fusion.4 = (f32[]{:T(128)}, f32[512,256]{1,0:T(8,128)S(1)}) fusion(f32[512,256]{1,0:T(8,128)S(1)} %get-tuple-element.344, f32[1,512,256]{2,1,0:T(8,128)S(1)} %get-tuple-element.334, f32[1,512,512]{2,1,0:T(8,128)S(1)} %get-tuple-element.343), kind=kOutput, calls=%fused_computation.12.clone.1 | convolution fusion | flops 805699584 | bytes 2621444 | tf_op jit(solution)/shard_map/while/body/...ij,...jk->...ik/dot_general | solution.py:12
  22.1 0.7 fusion.216
  24.5 1.4 %convolution_bitcast_fusion.6 = f32[1,512,256]{2,1,0:T(8,128)} fusion(f32[1,256,256]{2,1,0:T(8,128)S(1)} %get-tuple-element.158, f32[1,256,256]{2,1,0:T(8,128)S(1)} %get-tuple-element.160, f32[1,256,256]{2,1,0:T(8,128)S(1)} %get-tuple-element.159, f32[1,256,256]{1,2,0:T(8,128)S(1)} %get-tuple-element.157, f32[1,256,256]{1,2,0:T(8,128)S(1)} %get-tuple-element.156), kind=kOutput, calls=%fused_computation.62 | convolution fusion | flops 403570688 | bytes 1835008 | tf_op jit(solution)/shard_map/...ij,...jk->...ik/dot_general | solution.py:12
  26.6 2.4 %convolution_bitcast_fusion.10 = f32[1,512,256]{1,2,0:T(8,128)S(1)} fusion(f32[512,512]{1,0:T(8,128)S(1)} %maximum_maximum_fusion.1, f32[1,512,256]{2,1,0:T(8,128)} %collective-permute-done), kind=kOutput, calls=%fused_computation.66 | convolution fusion | flops 402653184 | bytes 2097152 | tf_op jit(solution)/shard_map/...ij,...jk->...ik/dot_general | solution.py:12
  30.3 0.8 copy-done.1
  34.2 1.6 %copy.61 = f32[1,512,512]{2,1,0:T(8,128)S(1)} copy(f32[1,512,512]{1,2,0:T(8,128)} %copy-done.1) | data formatting | bytes 2097152 | tf_op jit(solution)/shard_map/while | solution.py:71
  35.7 2.4 %convolution_bitcast_fusion.5 = f32[1,512,256]{1,2,0:T(8,128)S(1)} fusion(f32[512,512]{1,0:T(8,128)} %copy-done, f32[1,512,256]{2,1,0:T(8,128)} %collective-permute-done.1), kind=kOutput, calls=%fused_computation.61 | convolution fusion | flops 402653184 | bytes 2097152 | tf_op jit(solution)/shard_map/...ij,...jk->...ik/dot_general | solution.py:12
  38.2 0.9 slice_negate_fusion.4
  45.5 0.8 select_subtract_fusion.1
  47.9 1.0 %convolution_bitcast_fusion.7 = f32[1,512,256]{2,1,0:T(8,128)S(1)} fusion(f32[512,256]{0,1:T(8,128)S(1)} %select_subtract_fusion, f32[256,512]{0,1:T(8,128)S(1)} %get-tuple-element.218, f32[256,512]{0,1:T(8,128)S(1)} %get-tuple-element.217, f32[]{:T(128)} %bitcast.64), kind=kOutput, calls=%fused_computation.63 | convolution fusion | flops 403177472 | bytes 2097156 | tf_op jit(solution)/shard_map/...ij,...jk->...ik/dot_general | solution.py:12
  49.0 3.1 %while.25 = (f32[1,512,256]{2,1,0:T(8,128)S(1)}, f32[]{:T(128)}, s32[]{:T(128)}, f32[1,512,512]{2,1,0:T(8,128)S(1)}, f32[512,256]{1,0:T(8,128)S(1)}, /*index=5*/s32[]{:T(128)}) while((f32[1,512,256]{2,1,0:T(8,128)S(1)}, f32[]{:T(128)}, s32[]{:T(128)}, f32[1,512,512]{2,1,0:T(8,128)S(1)}, f32[512,256]{1,0:T(8,128)S(1)}, ...), condition=%wide.region_9.0_spmd, body=%wide.region_7.0_spmd.sunk | while | flops 1209335808 | bytes 6291549 | solution.py:71
  49.0 1.6 %multiply_reduce_fusion.5 = (f32[]{:T(128)}, f32[512,256]{1,0:T(8,128)S(1)}) fusion(f32[512,256]{1,0:T(8,128)S(1)} %get-tuple-element.362, f32[1,512,256]{2,1,0:T(8,128)S(1)} %get-tuple-element.352, f32[1,512,512]{2,1,0:T(8,128)S(1)} %get-tuple-element.361), kind=kOutput, calls=%fused_computation.27.clone.1 | convolution fusion | flops 805699584 | bytes 2621444 | tf_op jit(solution)/shard_map/while/body/...ij,...jk->...ik/dot_general | solution.py:12
  54.1 1.1 %convolution_bitcast_fusion.3 = f32[1,512,256]{1,2,0:T(8,128)S(1)} fusion(f32[1,256,256]{2,1,0:T(8,128)S(1)} %get-tuple-element.163, f32[1,256,256]{2,1,0:T(8,128)S(1)} %get-tuple-element.162, f32[1,256,256]{2,1,0:T(8,128)S(1)} %get-tuple-element.161, f32[1,256,256]{1,2,0:T(8,128)S(1)} %get-tuple-element.152, f32[1,256,256]{1,2,0:T(8,128)S(1)} %get-tuple-element.151), kind=kOutput, calls=%fused_computation.59 | convolution fusion | flops 806223872 | bytes 1835008 | tf_op jit(solution)/shard_map/...ij,...jk->...ik/dot_general | solution.py:12
  55.3 1.8 %convolution_bitcast_fusion.2 = f32[1,512,256]{2,1,0:T(8,128)S(1)} fusion(f32[1,256,256]{1,2,0:T(8,128)S(1)} %get-tuple-element.150, f32[1,256,256]{1,2,0:T(8,128)S(1)} %get-tuple-element.149, f32[1,256,256]{1,2,0:T(8,128)S(1)} %get-tuple-element.148, f32[1,256,256]{2,1,0:T(8,128)S(1)} %bitcast_negate_fusion, f32[1,256,256]{2,1,0:T(8,128)S(1)} %bitcast.397), kind=kOutput, calls=%fused_computation.58 | convolution fusion | flops 806223872 | bytes 1835008 | tf_op jit(solution)/shard_map/...ij,...jk->...ik/dot_general | solution.py:12
  57.3 32.5 %all_to_all.5 = f32[16,1,4,16,256]{4,3,2,1,0:T(8,128)S(1)} all-to-all(f32[16,1,4,16,256]{4,3,2,1,0:T(8,128)S(1)} %maximum_bitcast_fusion.18), channel_id=1, replica_groups=mesh['groups'=2,'energy'=8,'space'=2] {'energy','space'}, dimensions={0} | all-to-all | bytes 2097152 | tf_op jit(solution)/shard_map/all_to_all | solution.py:131
  90.5 0.8 copy.76
  (144 shorter events, 26.6 us)
Async XLA Ops:
  1.2 0.7 copy-start.12
  1.4 0.7 copy-start.11
  18.2 1.2 %copy-start.5 = (f32[512,256]{0,1:T(8,128)S(1)}, f32[512,256]{0,1:T(8,128)}, u32[]{:S(2)}) copy-start(f32[512,256]{0,1:T(8,128)} %select_subtract_fusion.7) | copy-start | bytes 1572868
  23.7 0.7 copy-start.13
  23.7 2.9 %collective-permute-start = (f32[1,512,256]{2,1,0:T(8,128)S(1)}, f32[1,512,256]{2,1,0:T(8,128)}, u32[]{:S(2)}, u32[]{:S(2)}) collective-permute-start(f32[1,512,256]{2,1,0:T(8,128)S(1)} %get-tuple-element.59), channel_id=1, source_target_pairs={{0,1},{1,0},{2,3},{3,2},{4,5},{5,4},{6,7},{7,6},{8,9},{9,8},{10,11... | collective-permute-start | bytes 1572872 | tf_op jit(solution)/shard_map/ppermute | solution.py:8
  24.5 1.5 %copy-start.2 = (f32[1,2,256,256]{3,2,1,0:T(8,128)S(1)}, f32[1,2,256,256]{3,2,1,0:T(8,128)}, u32[]{:S(2)}) copy-start(f32[1,2,256,256]{3,2,1,0:T(8,128)} %param.10) | copy-start | bytes 1572868
  25.9 9.8 %collective-permute-start.1 = (f32[1,512,256]{2,1,0:T(8,128)}, f32[1,512,256]{2,1,0:T(8,128)}, u32[]{:S(2)}, u32[]{:S(2)}) collective-permute-start(f32[1,512,256]{2,1,0:T(8,128)} %convolution_bitcast_fusion.6), channel_id=1, source_target_pairs={{0,1},{1,0},{2,3},{3,2},{4,5},{5,4},{6,7},{7,6},{8,9},{9,8},{10,11... | collective-permute-start | bytes 1572872 | tf_op jit(solution)/shard_map/ppermute | solution.py:8
  26.3 2.8 %copy-start.3 = (f32[256,256]{1,0:T(8,128)}, f32[256,256]{1,0:T(8,128)S(1)}, u32[]{:S(2)}) copy-start(f32[256,256]{1,0:T(8,128)S(1)} %get-tuple-element.212) | copy-start | bytes 786436
  26.4 2.8 %copy-start.9 = (f32[256,256]{0,1:T(8,128)}, f32[256,256]{0,1:T(8,128)S(1)}, u32[]{:S(2)}) copy-start(f32[256,256]{0,1:T(8,128)S(1)} %get-tuple-element.127) | copy-start | bytes 786436
  26.5 2.5 %copy-start = (f32[512,512]{1,0:T(8,128)}, f32[512,512]{1,0:T(8,128)S(1)}, u32[]{:S(2)}) copy-start(f32[512,512]{1,0:T(8,128)S(1)} %maximum_maximum_fusion.1) | copy-start | bytes 3145732
  30.0 1.0 %copy-start.1 = (f32[1,512,512]{1,2,0:T(8,128)}, f32[1,512,512]{1,2,0:T(8,128)S(1)}, u32[]{:S(2)}) copy-start(f32[1,512,512]{1,2,0:T(8,128)S(1)} %maximum_subtract_fusion.1) | copy-start | bytes 3145732
  52.1 1.0 %copy-start.7 = (f32[1,256,256]{1,2,0:T(8,128)S(1)}, f32[1,256,256]{1,2,0:T(8,128)}, u32[]{:S(2)}) copy-start(f32[1,256,256]{1,2,0:T(8,128)} %get-tuple-element.154) | copy-start | bytes 786436
  52.1 1.0 %copy-start.8 = (f32[1,256,256]{1,2,0:T(8,128)S(1)}, f32[1,256,256]{1,2,0:T(8,128)}, u32[]{:S(2)}) copy-start(f32[1,256,256]{1,2,0:T(8,128)} %get-tuple-element.155) | copy-start | bytes 786436
  52.1 1.1 %copy-start.10 = (f32[256,256]{0,1:T(8,128)S(1)}, f32[256,256]{0,1:T(8,128)}, u32[]{:S(2)}) copy-start(f32[256,256]{0,1:T(8,128)} %copy-done.9) | copy-start | bytes 786436
  52.3 1.0 %copy-start.4 = (f32[256,256]{1,0:T(8,128)S(1)}, f32[256,256]{1,0:T(8,128)}, u32[]{:S(2)}) copy-start(f32[256,256]{1,0:T(8,128)} %copy-done.3) | copy-start | bytes 786436
  52.3 1.1 %copy-start.6 = (f32[1,256,256]{1,2,0:T(8,128)S(1)}, f32[1,256,256]{1,2,0:T(8,128)}, u32[]{:S(2)}) copy-start(f32[1,256,256]{1,2,0:T(8,128)} %get-tuple-element.153) | copy-start | bytes 786436

commit v2 on v0

--- a/solution.py
+++ b/solution.py
@@ -99,20 +99,17 @@
     green_col = invert(system)
     g_re, g_im = split(green_col)
     scaled = embed(-g_im * source[:, None, :], g_re * source[:, None, :])
-    far_green = from_partner(green_col, "space", 0)
-    green_less = dot(scaled, stacked_adjoint(g_re, g_im))
-    far_less = from_partner(green_less, "space", 0)
-
     link = ham_coupling[0]
-    link_re = jnp.where(first, link[0], swap(link[0]))
-    link_im = jnp.where(first, link[1], -swap(link[1]))
+    link_re = jnp.where(first, swap(link[0]), link[0])
+    link_im = jnp.where(first, -swap(link[1]), link[1])
     link_embed = embed(link_re, link_im)
     link_adj = stacked_adjoint(link_re, link_im)
     high = lax.Precision.HIGH
-    left_green = dot(link_embed, far_green, high)
-    coupled_green = dot(embed(*split(left_green)), link_adj, high)
-    left_less = dot(link_embed, far_less, high)
-    coupled_less = dot(embed(*split(left_less)), link_adj, high)
+    left_green = dot(link_embed, green_col, high)
+    coupled_green = from_partner(dot(embed(*split(left_green)), link_adj, high), "space", 0)
+    green_less = dot(scaled, stacked_adjoint(g_re, g_im))
+    left_less = dot(link_embed, green_less, high)
+    coupled_less = from_partner(dot(embed(*split(left_less)), link_adj, high), "space", 0)
 
     full_re, full_im = split(invert(system - embed(*split(coupled_green))))
     less_re, less_im = split(coupled_less)

time: 90.8 us -> 84 us (0.925)
  local copies, waits for them, and re-layouts: 9.27 us -> 2.38 us
  other arithmetic: 8.14 us -> 9.51 us
  matrix products: 35.2 us -> 33.9 us
    unnamed x47 -> x24, local copies, waits for them, and re-layouts: 4.87 us -> 0.79 us
    while x3 -> x1, local copies, waits for them, and re-layouts: 2.08 us -> 0.19 us  [invert(): lax.while_loop(keep_going, newton, (approx, jnp.float32(jnp.inf), jnp.int...]
    dot_general x37, matrix products: 32.7 us -> 31.4 us  [dot(): return jnp.einsum('...ij,...jk->...ik', left, right, precision=precision)]
    slice x1, other arithmetic: 0.04 us -> 1.13 us  [split(): return (stacked[..., :order, :], stacked[..., order:, :])]
    slice x1 -> x0, local copies, waits for them, and re-layouts: 1.07 us -> none  [body(): imag_part = width[:, :, None] * identity - ham_diag[None, 0, 1]]
    concatenate x15 -> x14, other arithmetic: 2.33 us -> 2.44 us  [embed(): return jnp.concatenate([top, bottom], axis=-2)]
  transfers between devices with their start and end apart: 2 -> 2, of which waited for: 0 -> 0; matrix products, arithmetic and copies ran while one was open for 10% -> 23% of each run, Pallas kernels for 0% -> 0%
where the time goes in v2:
time: 84 us; the launch traced here: 83.8 us
  matrix products  33.9 us (40%)
  blocking collectives  32.4 us (39%)
  other arithmetic  9.51 us (11%)
  between operations  3.48 us (4%)
  local copies, waits for them, and re-layouts  2.38 us (3%)
  loops' own time  1.59 us (2%)
    all_to_all x1, blocking collectives, body(): lax.all_to_all(paired, ('energy', 'space'), split_axis=0, concat_axis=0,...  32.4 us
    dot_general x37, matrix products, dot(): return jnp.einsum('...ij,...jk->...ik', left, right, precision=precision)  31.4 us
    neg x23, other arithmetic, embed(): top = jnp.concatenate([real, -imag], axis=-1)  3.16 us
    concatenate x14, other arithmetic, embed(): return jnp.concatenate([top, bottom], axis=-2)  2.44 us
  transfers between devices with their start and end apart: 2, of which 0 were waited for; matrix products, arithmetic and copies ran while one was open for 23% of the time, Pallas kernels for 0%

profile of v2, /device:TPU:1, one launch (start us, length us, event | category | flops | bytes accessed | tf_op | source)
XLA Modules:
  0.0 83.8 jit_solution(15203689362108613018)
XLA Ops:
  0.1 0.7 copy-done.3
  0.7 1.2 %fusion.172 = (f32[1,256,256]{2,1,0:T(8,128)S(1)}, f32[1,256,256]{2,1,0:T(8,128)S(1)}, f32[1,256,256]{2,1,0:T(8,128)S(1)}) fusion(f32[1,2,256,256]{3,2,1,0:T(8,128)} %param.9, f32[256]{0:T(256)S(1)} %bitcast.399, f32[256]{0:T(256)S(1)} %bitcast.403, f32[]{:T(128)S(6)} %add.161), kind=kLoop, calls=%fused_computation.356 | loop fusion | flops 524288 | bytes 1312772 | tf_op jit(solution)/shard_map/neg | solution.py:20
  13.0 0.8 slice_negate_fusion.14
  13.8 1.4 %select_subtract_fusion.7 = f32[512,256]{0,1:T(8,128)} fusion(f32[512,256]{0,1:T(8,128)S(1)} %fusion.38, pred[256,256]{0,1:T(32,128)(4,1)S(1)} %iota_compare_fusion, f32[]{:T(128)} %bitcast.19, f32[1,256,256]{2,1,0:T(8,128)S(1)} %get-tuple-element.215, f32[1,256,256]{2,1,0:T(8,128)S(1)} %get-tuple-element.130, f32[1,256,256]{2,1,0:T(8,128)S(1)} %get-tuple-element.129), kind=kOutput, calls=%fused_computation.37 | convolution fusion | flops 403832832 | bytes 1900548 | tf_op jit(solution)/shard_map/...ij,...jk->...ik/dot_general | solution.py:12
  15.4 1.2 %maximum_bitcast_fusion.31 = (f32[256,512]{0,1:T(8,128)S(1)}, f32[256,512]{0,1:T(8,128)S(1)}) fusion(f32[1,256,256]{1,2,0:T(8,128)S(1)} %get-tuple-element.191, f32[1,256,256]{1,2,0:T(8,128)} %get-tuple-element.193, f32[1,256,256]{1,2,0:T(8,128)S(1)} %get-tuple-element.192), kind=kLoop, calls=%fused_computation.193 | loop fusion | flops 262144 | bytes 1835008 | tf_op jit(solution)/shard_map/concatenate | solution.py:22
  16.6 1.0 %convolution_bitcast_fusion.10 = f32[1,512,256]{2,1,0:T(8,128)S(1)} fusion(f32[512,256]{0,1:T(8,128)S(1)} %copy-done.1, f32[256,512]{0,1:T(8,128)S(1)} %get-tuple-element.231, f32[256,512]{0,1:T(8,128)S(1)} %get-tuple-element.230, f32[]{:T(128)} %bitcast.19), kind=kOutput, calls=%fused_computation.66 | convolution fusion | flops 403177472 | bytes 2097156 | tf_op jit(solution)/shard_map/...ij,...jk->...ik/dot_general | solution.py:12
  17.6 3.3 %while.24 = (f32[1,512,256]{2,1,0:T(8,128)S(1)}, f32[]{:T(128)}, s32[]{:T(128)}, f32[1,512,512]{2,1,0:T(8,128)S(1)}, f32[512,256]{1,0:T(8,128)S(1)}, /*index=5*/s32[]{:T(128)}) while((f32[1,512,256]{2,1,0:T(8,128)S(1)}, f32[]{:T(128)}, s32[]{:T(128)}, f32[1,512,512]{2,1,0:T(8,128)S(1)}, f32[512,256]{1,0:T(8,128)S(1)}, ...), condition=%wide.region_4.5_spmd, body=%wide.region_2.4_spmd.sunk | while | flops 1209335808 | bytes 6291549 | solution.py:71
  17.7 1.6 %multiply_reduce_fusion.4 = (f32[]{:T(128)}, f32[512,256]{1,0:T(8,128)S(1)}) fusion(f32[512,256]{1,0:T(8,128)S(1)} %get-tuple-element.344, f32[1,512,256]{2,1,0:T(8,128)S(1)} %get-tuple-element.334, f32[1,512,512]{2,1,0:T(8,128)S(1)} %get-tuple-element.343), kind=kOutput, calls=%fused_computation.12.clone.1 | convolution fusion | flops 805699584 | bytes 2621444 | tf_op jit(solution)/shard_map/while/body/...ij,...jk->...ik/dot_general | solution.py:12
  19.3 0.7 fusion.216
  21.4 1.0 %convolution_bitcast_fusion.9 = f32[1,512,256]{1,2,0:T(8,128)S(1)} fusion(f32[256,256]{1,0:T(8,128)S(1)} %get-tuple-element.212, f32[256,256]{1,0:T(8,128)S(1)} %get-tuple-element.128, f32[256,256]{1,0:T(8,128)S(1)} %neg.110, f32[1,512,256]{2,1,0:T(8,128)S(1)} %get-tuple-element.59), kind=kOutput, calls=%fused_computation.65 | convolution fusion | flops 403439616 | bytes 1835008 | tf_op jit(solution)/shard_map/...ij,...jk->...ik/dot_general | solution.py:12
  22.5 1.0 %convolution_bitcast_fusion.8 = f32[1,512,256]{2,1,0:T(8,128)S(1)} fusion(f32[1,256,256]{1,2,0:T(8,128)S(1)} %get-tuple-element.190, f32[1,256,256]{1,2,0:T(8,128)S(1)} %get-tuple-element.189, f32[1,256,256]{1,2,0:T(8,128)S(1)} %get-tuple-element.188, f32[256,256]{0,1:T(8,128)S(1)} %get-tuple-element.127, f32[256,256]{0,1:T(8,128)S(1)} %bitcast.397), kind=kOutput, calls=%fused_computation.64 | convolution fusion | flops 403570688 | bytes 1835008 | tf_op jit(solution)/shard_map/...ij,...jk->...ik/dot_general | solution.py:12
  23.8 1.0 %fusion.78 = f32[512,256]{1,0:T(8,128)S(1)} fusion(f32[1,256,256]{2,1,0:T(8,128)S(1)} %get-tuple-element.158, f32[1,256,256]{2,1,0:T(8,128)S(1)} %get-tuple-element.160, f32[1,256,256]{2,1,0:T(8,128)S(1)} %get-tuple-element.159, f32[1,256,256]{1,2,0:T(8,128)S(1)} %get-tuple-element.157, f32[1,256,256]{1,2,0:T(8,128)S(1)} %get-tuple-element.156), kind=kOutput, calls=%fused_computation.147 | convolution fusion | flops 806223872 | bytes 1835008 | tf_op jit(solution)/shard_map/...ij,...jk->...ik/dot_general | solution.py:12
  24.8 1.0 %convolution_bitcast_fusion.5 = f32[1,512,256]{1,2,0:T(8,128)S(1)} fusion(f32[512,256]{1,0:T(8,128)S(1)} %fusion.78, f32[256,256]{1,0:T(8,128)S(1)} %get-tuple-element.212, f32[256,256]{1,0:T(8,128)S(1)} %get-tuple-element.128, f32[256,256]{1,0:T(8,128)S(1)} %neg.110), kind=kOutput, calls=%fused_computation.61 | convolution fusion | flops 403439616 | bytes 1835008 | tf_op jit(solution)/shard_map/...ij,...jk->...ik/dot_general | solution.py:12
  25.9 1.8 %convolution_bitcast_fusion.4 = f32[1,512,256]{2,1,0:T(8,128)} fusion(f32[1,256,256]{1,2,0:T(8,128)S(1)} %get-tuple-element.155, f32[1,256,256]{1,2,0:T(8,128)S(1)} %get-tuple-element.154, f32[1,256,256]{1,2,0:T(8,128)S(1)} %get-tuple-element.153, f32[256,256]{0,1:T(8,128)S(1)} %get-tuple-element.127, f32[256,256]{0,1:T(8,128)S(1)} %bitcast.398), kind=kOutput, calls=%fused_computation.60 | convolution fusion | flops 403570688 | bytes 1835008 | tf_op jit(solution)/shard_map/...ij,...jk->...ik/dot_general | solution.py:12
  37.0 0.8 %select_subtract_fusion.2 = f32[512,256]{0,1:T(8,128)S(1)} fusion(f32[512,512]{1,0:T(8,128)S(1)} %maximum_subtract_fusion, f32[512,256]{0,1:T(8,128)S(1)} %fusion.61, pred[256,256]{0,1:T(32,128)(4,1)S(1)} %iota_compare_fusion, f32[]{:T(128)} %bitcast.66), kind=kOutput, calls=%fused_computation.32 | convolution fusion | flops 403046400 | bytes 2162692 | tf_op jit(solution)/shard_map/...ij,...jk->...ik/dot_general | solution.py:12
  40.9 1.0 %convolution_bitcast_fusion.6 = f32[1,512,256]{2,1,0:T(8,128)S(1)} fusion(f32[512,256]{0,1:T(8,128)S(1)} %select_subtract_fusion, f32[256,512]{0,1:T(8,128)S(1)} %get-tuple-element.217, f32[256,512]{0,1:T(8,128)S(1)} %get-tuple-element.216, f32[]{:T(128)} %bitcast.64), kind=kOutput, calls=%fused_computation.62 | convolution fusion | flops 403177472 | bytes 2097156 | tf_op jit(solution)/shard_map/...ij,...jk->...ik/dot_general | solution.py:12
  41.9 3.1 %while.25 = (f32[1,512,256]{2,1,0:T(8,128)S(1)}, f32[]{:T(128)}, s32[]{:T(128)}, f32[1,512,512]{2,1,0:T(8,128)S(1)}, f32[512,256]{1,0:T(8,128)S(1)}, /*index=5*/s32[]{:T(128)}) while((f32[1,512,256]{2,1,0:T(8,128)S(1)}, f32[]{:T(128)}, s32[]{:T(128)}, f32[1,512,512]{2,1,0:T(8,128)S(1)}, f32[512,256]{1,0:T(8,128)S(1)}, ...), condition=%wide.region_9.0_spmd, body=%wide.region_7.0_spmd.sunk | while | flops 1209335808 | bytes 6291549 | solution.py:71
  41.9 1.6 %multiply_reduce_fusion.5 = (f32[]{:T(128)}, f32[512,256]{1,0:T(8,128)S(1)}) fusion(f32[512,256]{1,0:T(8,128)S(1)} %get-tuple-element.362, f32[1,512,256]{2,1,0:T(8,128)S(1)} %get-tuple-element.352, f32[1,512,512]{2,1,0:T(8,128)S(1)} %get-tuple-element.361), kind=kOutput, calls=%fused_computation.27.clone.1 | convolution fusion | flops 805699584 | bytes 2621444 | tf_op jit(solution)/shard_map/while/body/...ij,...jk->...ik/dot_general | solution.py:12
  43.6 0.7 fusion.218
  45.4 1.1 %fusion.173 = (f32[1,256,256]{2,1,0:T(8,128)S(1)}, f32[1,256,256]{2,1,0:T(8,128)S(1)}) fusion(f32[1,512,256]{2,1,0:T(8,128)} %collective-permute-done.1, f32[256]{0:T(256)S(1)} %mul.777), kind=kLoop, calls=%fused_computation.357 | loop fusion | flops 196608 | bytes 1049600 | tf_op jit(solution)/shard_map/slice | solution.py:31
  46.5 1.1 %convolution_bitcast_fusion.3 = f32[1,512,256]{1,2,0:T(8,128)S(1)} fusion(f32[1,256,256]{2,1,0:T(8,128)S(1)} %get-tuple-element.163, f32[1,256,256]{2,1,0:T(8,128)S(1)} %get-tuple-element.162, f32[1,256,256]{2,1,0:T(8,128)S(1)} %get-tuple-element.161, f32[1,256,256]{2,1,0:T(8,128)S(1)} %get-tuple-element.152, f32[1,256,256]{2,1,0:T(8,128)S(1)} %get-tuple-element.151), kind=kOutput, calls=%fused_computation.59 | convolution fusion | flops 806223872 | bytes 1835008 | tf_op jit(solution)/shard_map/...ij,...jk->...ik/dot_general | solution.py:12
  47.7 1.8 %convolution_bitcast_fusion.2 = f32[1,512,256]{2,1,0:T(8,128)S(1)} fusion(f32[1,256,256]{1,2,0:T(8,128)S(1)} %get-tuple-element.150, f32[1,256,256]{1,2,0:T(8,128)S(1)} %get-tuple-element.149, f32[1,256,256]{1,2,0:T(8,128)S(1)} %get-tuple-element.148, f32[1,256,256]{2,1,0:T(8,128)S(1)} %bitcast_negate_fusion, f32[1,256,256]{2,1,0:T(8,128)S(1)} %bitcast.390), kind=kOutput, calls=%fused_computation.58 | convolution fusion | flops 806223872 | bytes 1835008 | tf_op jit(solution)/shard_map/...ij,...jk->...ik/dot_general | solution.py:12
  49.8 32.4 %all_to_all.5 = f32[16,1,4,16,256]{4,3,2,1,0:T(8,128)S(1)} all-to-all(f32[16,1,4,16,256]{4,3,2,1,0:T(8,128)S(1)} %maximum_bitcast_fusion.18), channel_id=1, replica_groups=mesh['groups'=2,'energy'=8,'space'=2] {'energy','space'}, dimensions={0} | all-to-all | bytes 2097152 | tf_op jit(solution)/shard_map/all_to_all | solution.py:128
  82.9 0.8 %copy.58 = f32[8,2,2,16,256]{4,3,2,1,0:T(8,128)} copy(f32[8,2,2,16,256]{4,3,1,2,0:T(8,128)S(1)} %pad_maximum_fusion.1) | data formatting | bytes 1048576 | tf_op jit(solution)/shard_map/stack | solution.py:145
  (119 shorter events, 22.8 us)
Async XLA Ops:
  0.0 0.7 copy-start.3
  0.1 0.7 copy-start.2
  15.4 1.2 %copy-start.1 = (f32[512,256]{0,1:T(8,128)S(1)}, f32[512,256]{0,1:T(8,128)}, u32[]{:S(2)}) copy-start(f32[512,256]{0,1:T(8,128)} %select_subtract_fusion.7) | copy-start | bytes 1572868
  17.6 3.3 %copy-start = (f32[1,2,256,256]{3,2,1,0:T(8,128)S(1)}, f32[1,2,256,256]{3,2,1,0:T(8,128)}, u32[]{:S(2)}) copy-start(f32[1,2,256,256]{3,2,1,0:T(8,128)} %param.10) | copy-start | bytes 1572868
  22.5 1.1 %copy-start.4 = (f32[1,1,256]{2,1,0:T(1,128)S(1)}, f32[1,1,256]{2,1,0:T(1,128)}, u32[]{:S(2)}) copy-start(f32[1,1,256]{2,1,0:T(1,128)} %param.13) | copy-start | bytes 3076
  23.5 4.6 %collective-permute-start = (f32[1,512,256]{2,1,0:T(8,128)S(1)}, f32[1,512,256]{2,1,0:T(8,128)S(1)}, u32[]{:S(2)}, u32[]{:S(2)}) collective-permute-start(f32[1,512,256]{2,1,0:T(8,128)S(1)} %convolution_bitcast_fusion.8), channel_id=1, source_target_pairs={{0,1},{1,0},{2,3},{3,2},{4,5},{5,4},{6,7},{7,6},{8,9},{9,8},{10,11... | collective-permute-start | bytes 1572872 | tf_op jit(solution)/shard_map/ppermute | solution.py:8
  27.7 17.7 %collective-permute-start.1 = (f32[1,512,256]{2,1,0:T(8,128)}, f32[1,512,256]{2,1,0:T(8,128)}, u32[]{:S(2)}, u32[]{:S(2)}) collective-permute-start(f32[1,512,256]{2,1,0:T(8,128)} %convolution_bitcast_fusion.4), channel_id=1, source_target_pairs={{0,1},{1,0},{2,3},{3,2},{4,5},{5,4},{6,7},{7,6},{8,9},{9,8},{10,11... | collective-permute-start | bytes 1572872 | tf_op jit(solution)/shard_map/ppermute | solution.py:8
